TPU v7x, 128 devices: a whole 4x4x4 slice. The times are simulated.
128 devices in a mesh: layer: 16 (over y, x), prow: 4 (over z), pcol: 2 (over core).
Axes of the slice: x: 4, y: 4, z: 4, core: 2. Of those that a mesh axis runs over, the one named last changes fastest.
Arguments:
- front: bfloat16 [16, 2048, 32768], P('layer', 'prow', 'pcol'), may hold values from -6 to 6
- pivots: bfloat16 [16, 2, 256, 32768], P('layer', None, 'prow', 'pcol'), may hold values from -0.8984375 to 0.8984375
- inverses: bfloat16 [16, 2, 256, 256], P('layer'), may hold values from -0.1875 to 0.1875
- slab_pattern: int32 [16, 8, 128], P('layer', 'prow', 'pcol'), may hold values 0 or 1
- pivot_pattern: int32 [16, 2, 128], P('layer', None, 'pcol'), may hold values from 0 to 1, as said below
Outputs:
- ancestor: float32 [4, 16, 32, 32768], P('prow', 'layer', None, 'pcol')
- lower: bfloat16 [16, 2048, 512], P('layer', 'prow')
- upper: bfloat16 [16, 256, 32768], P('layer', 'prow', 'pcol')
Inputs may be any that keep to these rules, and one draw needn't show every extreme that they name: `pivot_pattern`: each entry says whether that block of the pivot rows is structurally nonzero. `slab_pattern`: each entry says whether that block of the front rows is structurally nonzero.
All inputs are finite; a program needn't handle non-finite values.
Results may differ from a plain program's by a relative error of at most 0.014.
Values may be sent and summed in bfloat16 or wider, within the bound.
No kernel may reach another device: no remote copies, remote signals or barrier semaphores. Data moves between devices by JAX's collectives and lax.ppermute only.
A program may use at most 192 MiB of HBM per device.

v0:
```python
import jax
import jax.numpy as jnp
from jax import lax
from jax.sharding import PartitionSpec as P


def ring(value, axis, size, step):
    return lax.ppermute(value, axis, [(i, (i + step) % size) for i in range(size)])


def gather_relative(value, axis, size):
    from_prev = ring(value, axis, size, 1)
    from_next = ring(value, axis, size, -1)
    half = value.shape[1] // 2
    far_lo = ring(from_prev[:, :half], axis, size, 1)
    far_hi = ring(from_next[:, half:], axis, size, -1)
    far = jnp.concatenate([far_lo, far_hi], 1)
    return jnp.concatenate([value, from_next, far, from_prev], 1)


def grid_shift(value, axis, side, dy, dx):
    pairs = []
    for y in range(side):
        for x in range(side):
            pairs.append((y * side + x, (y + dy) % side * side + (x + dx) % side))
    return lax.ppermute(value, axis, pairs)


def ring_reduce(blocks, send):
    half = blocks.shape[1] // 2
    far = blocks[2].astype(jnp.bfloat16)
    fwd1 = send(far[:half], 1)
    bwd1 = send(far[half:], -1)
    next_block = blocks[1]
    prev_block = blocks[3]
    fwd2 = send(
        jnp.concatenate(
            [next_block[:half] + fwd1.astype(jnp.float32), next_block[half:]], 0
        ).astype(jnp.bfloat16),
        1,
    )
    bwd2 = send(
        jnp.concatenate(
            [prev_block[:half], prev_block[half:] + bwd1.astype(jnp.float32)], 0
        ).astype(jnp.bfloat16),
        -1,
    )
    return blocks[0] + fwd2.astype(jnp.float32) + bwd2.astype(jnp.float32)


def relative(value, own, axis):
    return jnp.stack(
        [lax.dynamic_index_in_dim(value, (own + j) % 4, axis, keepdims=False) for j in range(4)], 0
    )


def grid_reduce_scatter(left, right, axis):
    side = 4
    index = lax.axis_index(axis)
    gy = index // side
    gx = index % side
    rows, width = left.shape
    part = rows // (side * side)
    left = left.reshape(side, side, part, width)
    right = right.reshape(side, side, part, width)

    def along_x(v, step):
        return grid_shift(v, axis, side, 0, step)

    def along_y(v, step):
        return grid_shift(v, axis, side, step, 0)

    left = ring_reduce(relative(left, gx, 1), along_x)
    left = ring_reduce(relative(left, gy, 0), along_y)
    right = ring_reduce(relative(right, gy, 0), along_y)
    right = ring_reduce(relative(right, gx, 0), along_x)
    return jnp.concatenate([left, right], 1)


def on_device(front, pivots, inverses, slab_pattern, pivot_pattern):
    block_size = inverses.shape[-1]
    panel_width = 2 * block_size
    row_count = front.shape[1]
    col_count = front.shape[2]
    own_rows = pivots.shape[2]
    masked = (
        front[0].reshape(row_count // block_size, block_size, col_count // block_size, block_size)
        * slab_pattern[0].astype(jnp.bfloat16)[:, None, :, None]
    ).reshape(row_count, col_count)

    def mask_pivots(lo, hi):
        return (
            pivots[0, :, :, lo:hi].reshape(2, own_rows, (hi - lo) // block_size, block_size)
            * pivot_pattern[0, :, lo // block_size : hi // block_size].astype(jnp.bfloat16)[
                :, None, :, None
            ]
        ).reshape(2, own_rows, hi - lo)

    first_inverse = inverses[0, 0]
    second_inverse = inverses[0, 1]
    row_offset = lax.axis_index("prow") * own_rows
    pcol = lax.axis_index("pcol")
    n_prow = lax.axis_size("prow")
    n_pcol = lax.axis_size("pcol")
    assert n_prow == 4
    half = col_count * 11 // 16 // block_size * block_size
    first_cols = mask_pivots(0, half)
    gathered = lax.all_gather(first_cols, "prow", axis=1, tiled=True)
    later_cols, gathered = lax.optimization_barrier((mask_pivots(half, col_count), gathered))
    panel = jnp.roll(
        gather_relative(first_cols[:, :, :panel_width], "prow", n_prow), row_offset, axis=1
    )
    front_cols = masked[:, :panel_width]
    pivot_cols = panel[0]
    second_cols = panel[1]
    lower_pivot = jnp.dot(
        second_cols[:, :block_size], first_inverse, preferred_element_type=jnp.float32
    ).astype(jnp.bfloat16)
    lower_first = jnp.dot(
        front_cols[:, :block_size], first_inverse, preferred_element_type=jnp.float32
    ).astype(jnp.bfloat16)
    carried = (
        front_cols[:, block_size:].astype(jnp.float32)
        - jnp.dot(
            lower_first, pivot_cols[:, block_size:panel_width], preferred_element_type=jnp.float32
        )
    ).astype(jnp.bfloat16)
    lower_second = jnp.dot(carried, second_inverse, preferred_element_type=jnp.float32).astype(
        jnp.bfloat16
    )
    lower_panel = jnp.concatenate([lower_first, lower_second], 1)
    sent = lax.ppermute((lower_panel, lower_pivot), "pcol", [(0, i) for i in range(1, n_pcol)])
    on_root = pcol == 0
    lower_panel = jnp.where(on_root, lower_panel, sent[0])
    lower_pivot = jnp.where(on_root, lower_pivot, sent[1])
    folded = (
        lower_panel[:, :block_size].astype(jnp.float32)
        - jnp.dot(lower_panel[:, block_size:], lower_pivot, preferred_element_type=jnp.float32)
    ).astype(jnp.bfloat16)
    multipliers = jnp.concatenate([folded, lower_panel[:, block_size:]], 1)
    multipliers_rel = jnp.concatenate(
        [
            jnp.roll(folded, -row_offset, axis=1),
            jnp.roll(lower_panel[:, block_size:], -row_offset, axis=1),
        ],
        1,
    )
    col_index = pcol * col_count + jnp.arange(col_count, dtype=jnp.int32)
    retained = col_index >= panel_width
    schur_first = masked[:, :half].astype(jnp.float32) - jnp.dot(
        multipliers, gathered.reshape(2 * block_size, half), preferred_element_type=jnp.float32
    )
    schur_first = jnp.where(retained[None, :half], schur_first, jnp.zeros_like(schur_first))
    second_half = later_cols
    schur_first = schur_first.astype(jnp.bfloat16)
    summed_first = lax.psum_scatter(schur_first, "layer", scatter_dimension=0, tiled=True).astype(
        jnp.float32
    )
    gathered_rel = gather_relative(second_half, "prow", n_prow)
    own_pivot = lax.dynamic_slice_in_dim(lower_pivot, row_offset, own_rows, 0)
    upper_own = jnp.concatenate(
        [
            (
                first_cols[1].astype(jnp.float32)
                - jnp.dot(own_pivot, gathered[0], preferred_element_type=jnp.float32)
            ).astype(jnp.bfloat16),
            (
                later_cols[1].astype(jnp.float32)
                - jnp.dot(
                    jnp.roll(own_pivot, -row_offset, axis=1),
                    gathered_rel[0],
                    preferred_element_type=jnp.float32,
                )
            ).astype(jnp.bfloat16),
        ],
        1,
    )
    split = (col_count - half) // 2
    stacked_rel = gathered_rel.reshape(2 * block_size, col_count - half)
    schur_halves = []
    for start in (0, split):
        cols = slice(half + start, half + start + split)
        schur_half = masked[:, cols].astype(jnp.float32) - jnp.dot(
            multipliers_rel,
            stacked_rel[:, start : start + split],
            preferred_element_type=jnp.float32,
        )
        schur_halves.append(jnp.where(retained[None, cols], schur_half, jnp.zeros_like(schur_half)))
    summed = jnp.concatenate([summed_first, grid_reduce_scatter(*schur_halves, "layer")], 1)
    ancestor = summed.reshape(1, 1, summed.shape[0], col_count)
    return (ancestor, lower_panel[None], upper_own[None])


def solution(mesh):
    placed = (
        P("layer", "prow", "pcol"),
        P("layer", None, "prow", "pcol"),
        P("layer", None, None, None),
        P("layer", "prow", "pcol"),
        P("layer", None, "pcol"),
    )
    return jax.shard_map(
        on_device,
        mesh=mesh,
        in_specs=placed,
        out_specs=(
            P("prow", "layer", None, "pcol"),
            P("layer", "prow", None),
            P("layer", "prow", "pcol"),
        ),
        check_vma=False,
    )
```

profile of v0, /device:TPU:1, one launch (start us, length us, event | category | flops | bytes accessed | tf_op | source)
XLA Modules:
  0.0 258.3 jit_solution(1569205453357182786)
XLA Ops:
  7.2 0.7 convert.70
  8.0 3.6 %bitcast_multiply_fusion.1 = bf16[2,64,11264]{2,1,0:T(8,128)(2,1)} fusion(bf16[2,11264]{1,0:T(2,128)(2,1)S(1)} %bitcast.177, bf16[1,2,64,16384]{3,2,1,0:T(8,128)(2,1)} %param.8), kind=kLoop, calls=%fused_computation.10 | loop fusion | flops 1441792 | bytes 5812224 | tf_op jit(solution)/shard_map/mul | solution.py:93
  11.7 1.6 fusion.61
  13.3 4.6 %collective-permute-start = (bf16[2,64,512]{2,1,0:T(8,128)(2,1)S(1)}, bf16[2,64,512]{2,1,0:T(8,128)(2,1)S(1)}, u32[]{:S(2)}, u32[]{:S(2)}) collective-permute-start(bf16[2,64,512]{2,1,0:T(8,128)(2,1)S(1)} %get-tuple-element.20), channel_id=1, source_target_pairs={{0,6},{2,0},{4,2},{6,4},{1,7},{3,1},{5,3},{7,5},{8,14},{10,8},{12,... | collective-permute-start | bytes 393224 | tf_op jit(solution)/shard_map/ppermute | solution.py:8
  18.1 3.0 %reshape_squeeze.14 = bf16[2,64,44,256]{3,2,1,0:T(8,128)(2,1)} reshape(bf16[1,2,64,11264]{3,2,1,0:T(8,128)(2,1)S(1)} %slice-done) | data formatting | bytes 5767168 | tf_op jit(solution)/shard_map/reshape;squeeze | solution.py:93
  21.1 1.7 fusion.6
  22.7 1.6 copy.19
  24.4 2.7 %mul.48 = bf16[2,256,64,256]{3,2,1,0:T(8,128)(2,1)S(1)} broadcast(bf16[2,64]{1,0:T(2,128)(2,1)S(1)} %convert_bitcast_fusion), dimensions={0,2} | broadcast | bytes 16777472 | tf_op jit(solution)/shard_map/mul | solution.py:87
  27.2 12.4 %copy.16 = bf16[64,8,64,256]{3,1,2,0:T(8,128)(2,1)} copy(bf16[64,8,64,256]{3,2,1,0:T(8,128)(2,1)S(1)} %bitcast.163) | data formatting | bytes 33554432
  39.7 2.5 bitcast_multiply_fusion.2
  42.2 12.2 %bitcast_multiply_fusion = bf16[512,16384]{1,0:T(8,128)(2,1)S(1)} fusion(bf16[512,16384]{1,0:T(8,128)(2,1)} %bitcast.162, bf16[1,512,16384]{2,1,0:T(8,128)(2,1)} %param.7), kind=kLoop, calls=%fused_computation.1 | loop fusion | flops 8388608 | bytes 50331648 | tf_op jit(solution)/shard_map/mul | solution.py:87
  54.4 5.8 %copy-done = bf16[512,16384]{1,0:T(8,128)(2,1)} copy-done((bf16[512,16384]{1,0:T(8,128)(2,1)}, bf16[512,16384]{1,0:T(8,128)(2,1)S(1)}, u32[]{:S(2)}) %copy-start) | copy-done | bytes 16777240
  60.6 2.7 %collective-permute-start.3 = (bf16[2,32,512]{2,1,0:T(8,128)(2,1)S(1)}, bf16[2,32,512]{2,1,0:T(8,128)(2,1)S(1)}, u32[]{:S(2)}, u32[]{:S(2)}) collective-permute-start(bf16[2,32,512]{2,1,0:T(8,128)(2,1)S(1)} %slice.338), channel_id=1, source_target_pairs={{0,6},{2,0},{4,2},{6,4},{1,7},{3,1},{5,3},{7,5},{8,14},{10,8},{12,... | collective-permute-start | bytes 196616 | tf_op jit(solution)/shard_map/ppermute | solution.py:8
  63.4 3.6 %collective-permute-done.2 = bf16[2,32,512]{2,1,0:T(8,128)(2,1)S(1)} collective-permute-done((bf16[2,32,512]{2,1,0:T(8,128)(2,1)S(1)}, bf16[2,32,512]{2,1,0:T(8,128)(2,1)S(1)}, u32[]{:S(2)}, u32[]{:S(2)}) %collective-permute-start.2) | collective-permute-done | bytes 65568 | tf_op jit(solution)/shard_map/ppermute | solution.py:8
  67.0 0.9 constant_dynamic-update-slice_fusion.4
  68.0 0.7 dynamic-slice_bitcast_fusion.4
  68.9 1.3 collective-permute-start.5
  70.2 1.5 convolution_convert_fusion
  71.8 1.3 collective-permute-start.4
  73.7 0.9 broadcast_select_fusion.1
  74.7 0.6 copy-done.7
  75.3 1.5 collective-permute-done.4
  76.8 1.2 broadcast_select_fusion
  78.0 0.7 slice.341
  78.7 1.0 copy.12
  79.7 1.9 subtract_convert_fusion
  81.6 44.8 %all-gather.2.cloned.1.call-done = bf16[2,256,11264]{2,1,0:T(8,128)(2,1)} async-done(((bf16[2,64,11264]{2,1,0:T(8,128)(2,1)}), bf16[2,256,11264]{2,1,0:T(8,128)(2,1)}) %all-gather.2.cloned.1.call-update) | async-done | bytes 11534352 | tf_op jit(solution)/shard_map/all_gather | solution.py:108
  126.4 0.9 collective-permute-start.6
  127.8 13.9 %select_convert_fusion = bf16[512,11264]{1,0:T(8,128)(2,1)} fusion(bf16[512,11264]{1,0:T(8,128)(2,1)} %bitcast.176, bf16[512,16384]{1,0:T(8,128)(2,1)} %copy-done, pred[11264]{0:T(1024)(128)(4,1)S(1)} %slice-done.1, bf16[512,256]{0,1:T(8,128)(2,1)} %slice.341, bf16[512,256]{0,1:T(8,128)(2,1)} %subtract_convert_fusion), kind=kOutput, calls=%fused_computation | convolution fusion | flops 5929697280 | bytes 35138560 | tf_op jit(solution)/shard_map/dot_general | solution.py:150
  141.7 0.9 copy-done.3
  142.6 1.4 fusion.25
  144.0 1.4 constant_dynamic-update-slice_fusion.14
  145.4 12.5 %collective-permute-done.7 = bf16[2,64,5120]{2,1,0:T(8,128)(2,1)} collective-permute-done((bf16[2,64,5120]{2,1,0:T(8,128)(2,1)}, bf16[2,64,5120]{2,1,0:T(8,128)(2,1)}, u32[]{:S(2)}, u32[]{:S(2)}) %collective-permute-start.7) | collective-permute-done | bytes 1310752 | tf_op jit(solution)/shard_map/ppermute | solution.py:8
  157.9 1.1 slice.345
  159.2 3.9 %fusion = bf16[64,11264]{1,0:T(8,128)(2,1)S(1)} fusion(f32[64,11264]{1,0:T(8,128)S(1)} %bitcast.165, bf16[64,256]{1,0:T(8,128)(2,1)S(1)} %constant_dynamic-slice_fusion, bf16[2,256,11264]{2,1,0:T(8,128)(2,1)} %all-gather.2.cloned.1.call-done), kind=kOutput, calls=%fused_computation.3 | convolution fusion | flops 370540544 | bytes 10125312 | tf_op jit(solution)/shard_map/dot_general | solution.py:165
  163.1 1.1 slice.346
  164.2 2.7 %collective-permute-start.9 = (bf16[2,32,5120]{2,1,0:T(8,128)(2,1)S(1)}, bf16[2,32,5120]{2,1,0:T(8,128)(2,1)S(1)}, u32[]{:S(2)}, u32[]{:S(2)}) collective-permute-start(bf16[2,32,5120]{2,1,0:T(8,128)(2,1)S(1)} %slice.346), channel_id=1, source_target_pairs={{0,6},{2,0},{4,2},{6,4},{1,7},{3,1},{5,3},{7,5},{8,14},{10,8},{12,... | collective-permute-start | bytes 1966088 | tf_op jit(solution)/shard_map/ppermute | solution.py:8
  166.9 1.5 constant_dynamic-update-slice_fusion.13
  168.5 6.2 %collective-permute-done.8 = bf16[2,32,5120]{2,1,0:T(8,128)(2,1)S(1)} collective-permute-done((bf16[2,32,5120]{2,1,0:T(8,128)(2,1)S(1)}, bf16[2,32,5120]{2,1,0:T(8,128)(2,1)S(1)}, u32[]{:S(2)}, u32[]{:S(2)}) %collective-permute-start.8) | collective-permute-done | bytes 655392 | tf_op jit(solution)/shard_map/ppermute | solution.py:8
  174.7 4.1 %collective-permute-done.9 = bf16[2,32,5120]{2,1,0:T(8,128)(2,1)S(1)} collective-permute-done((bf16[2,32,5120]{2,1,0:T(8,128)(2,1)S(1)}, bf16[2,32,5120]{2,1,0:T(8,128)(2,1)S(1)}, u32[]{:S(2)}, u32[]{:S(2)}) %collective-permute-start.9) | collective-permute-done | bytes 655392 | tf_op jit(solution)/shard_map/ppermute | solution.py:8
  178.8 1.5 constant_dynamic-update-slice_fusion.10
  180.4 3.6 %subtract_select_fusion.1 = f32[512,2560]{1,0:T(8,128)S(1)} fusion(bf16[512,5120]{1,0:T(8,128)(2,1)S(1)} %bitcast.174, bf16[512,16384]{1,0:T(8,128)(2,1)} %copy-done, pred[2560]{0:T(1024)(128)(4,1)S(1)} %copy-done.10, bf16[512,256]{0,1:T(8,128)(2,1)S(1)} %get-tuple-element.42, bf16[512,256]{0,1:T(8,128)(2,1)S(1)} %get-tuple-element.43), kind=kOutput, calls=%fused_computation.9 | convolution fusion | flops 1347158016 | bytes 11013120 | tf_op jit(solution)/shard_map/dot_general | solution.py:183
  184.1 1.8 collective-permute-start.10
  185.9 1.1 collective-permute-start.12
  187.1 3.5 %subtract_select_fusion = f32[512,2560]{1,0:T(8,128)S(1)} fusion(bf16[512,5120]{1,0:T(8,128)(2,1)S(1)} %bitcast.175, bf16[512,16384]{1,0:T(8,128)(2,1)} %copy-done, pred[2560]{0:T(1024)(128)(4,1)S(1)} %copy-done.9, bf16[512,256]{0,1:T(8,128)(2,1)S(1)} %get-tuple-element.42, bf16[512,256]{0,1:T(8,128)(2,1)S(1)} %get-tuple-element.43), kind=kOutput, calls=%fused_computation.8 | convolution fusion | flops 1347158016 | bytes 11013120 | tf_op jit(solution)/shard_map/dot_general | solution.py:183
  190.7 1.6 collective-permute-start.18
  192.3 1.2 collective-permute-start.20
  193.5 0.7 fusion.1
  194.5 1.5 maximum_bitcast_fusion.1
  196.0 5.0 %collective-permute-done.10 = bf16[2,32,2560]{2,1,0:T(8,128)(2,1)S(1)} collective-permute-done((bf16[2,32,2560]{2,1,0:T(8,128)(2,1)S(1)}, bf16[2,32,2560]{2,1,0:T(8,128)(2,1)S(1)}, u32[]{:S(2)}, u32[]{:S(2)}) %collective-permute-start.10) | collective-permute-done | bytes 327712 | tf_op jit(solution)/shard_map/ppermute | solution.py:26
  201.1 1.0 collective-permute-start.11
  202.3 2.0 collective-permute-start.13
  204.3 2.4 collective-permute-done.18
  207.1 2.7 %collective-permute-start.21 = (bf16[4,32,2560]{2,1,0:T(8,128)(2,1)S(1)}, bf16[4,32,2560]{2,1,0:T(8,128)(2,1)S(1)}, u32[]{:S(2)}, u32[]{:S(2)}) collective-permute-start(bf16[4,32,2560]{2,1,0:T(8,128)(2,1)S(1)} %pad_maximum_fusion.3), channel_id=1, source_target_pairs={{0,96},{8,104},{16,112},{24,120},{32,0},{40,8},{48,16},{56,24},{64... | collective-permute-start | bytes 1966088 | tf_op jit(solution)/shard_map/ppermute | solution.py:26
  209.8 15.2 %collective-permute-done.11 = bf16[4,32,2560]{2,1,0:T(8,128)(2,1)S(1)} collective-permute-done((bf16[4,32,2560]{2,1,0:T(8,128)(2,1)S(1)}, bf16[4,32,2560]{2,1,0:T(8,128)(2,1)S(1)}, u32[]{:S(2)}, u32[]{:S(2)}) %collective-permute-start.11) | collective-permute-done | bytes 655392 | tf_op jit(solution)/shard_map/ppermute | solution.py:26
  225.6 2.4 collective-permute-start.16
  228.8 2.4 collective-permute-start.24
  231.4 3.3 %collective-permute-start.17 = (bf16[32,2560]{1,0:T(8,128)(2,1)S(1)}, bf16[32,2560]{1,0:T(8,128)(2,1)S(1)}, u32[]{:S(2)}, u32[]{:S(2)}) collective-permute-start(bf16[32,2560]{1,0:T(8,128)(2,1)S(1)} %pad_maximum_fusion.11), channel_id=1, source_target_pairs={{0,96},{8,104},{16,112},{24,120},{32,0},{40,8},{48,16},{56,24},{64... | collective-permute-start | bytes 491528 | tf_op jit(solution)/shard_map/ppermute | solution.py:26
  235.3 2.6 %collective-permute-start.25 = (bf16[32,2560]{1,0:T(8,128)(2,1)S(1)}, bf16[32,2560]{1,0:T(8,128)(2,1)S(1)}, u32[]{:S(2)}, u32[]{:S(2)}) collective-permute-start(bf16[32,2560]{1,0:T(8,128)(2,1)S(1)} %pad_maximum_fusion.13), channel_id=1, source_target_pairs={{0,24},{8,0},{16,8},{24,16},{32,56},{40,32},{48,40},{56,48},{64,88... | collective-permute-start | bytes 491528 | tf_op jit(solution)/shard_map/ppermute | solution.py:26
  237.9 2.6 %collective-permute-done.15 = bf16[32,2560]{1,0:T(8,128)(2,1)S(1)} collective-permute-done((bf16[32,2560]{1,0:T(8,128)(2,1)S(1)}, bf16[32,2560]{1,0:T(8,128)(2,1)S(1)}, u32[]{:S(2)}, u32[]{:S(2)}) %collective-permute-start.15) | collective-permute-done | bytes 163872 | tf_op jit(solution)/shard_map/ppermute | solution.py:26
  240.9 3.8 %collective-permute-done.23 = bf16[32,2560]{1,0:T(8,128)(2,1)S(1)} collective-permute-done((bf16[32,2560]{1,0:T(8,128)(2,1)S(1)}, bf16[32,2560]{1,0:T(8,128)(2,1)S(1)}, u32[]{:S(2)}, u32[]{:S(2)}) %collective-permute-start.23) | collective-permute-done | bytes 163872 | tf_op jit(solution)/shard_map/ppermute | solution.py:26
  244.7 4.1 %reduce-scatter.2.cloned.1.call-done = bf16[32,11264]{1,0:T(8,128)(2,1)} async-done(((bf16[512,11264]{1,0:T(8,128)(2,1)}), bf16[32,11264]{1,0:T(8,128)(2,1)}) %reduce-scatter.2.cloned.1.call-update) | async-done | bytes 720912 | tf_op jit(solution)/shard_map/reduce_scatter | solution.py:156
  248.8 1.2 convert_element_type.165
  250.0 1.5 maximum_bitcast_fusion
  (111 shorter events, 6.0 us)
Async XLA Ops:
  7.2 119.2 %all-gather.2.cloned.1.call-start = ((), (), s32[]{:S(2)}) async-start(), calls=%async_computation.1 | async-start | bytes 14417920 | tf_op jit(solution)/shard_map/all_gather | solution.py:108
  11.7 237.2 %reduce-scatter.2.cloned.1.call-start = ((), (), s32[]{:S(2)}) async-start(), calls=%async_computation.2 | async-start | bytes 12255232 | tf_op jit(solution)/shard_map/reduce_scatter | solution.py:156
  13.3 4.8 %slice-start = ((bf16[1,2,64,16384]{3,2,1,0:T(8,128)(2,1)}), bf16[1,2,64,11264]{3,2,1,0:T(8,128)(2,1)S(1)}, s32[]{:S(2)}) async-start(bf16[1,2,64,16384]{3,2,1,0:T(8,128)(2,1)} %param.8), calls=%async_computation.3 | async-start | bytes 5767168 | tf_op jit(solution)/shard_map/slice | solution.py:93
  13.3 47.3 %collective-permute-start = (bf16[2,64,512]{2,1,0:T(8,128)(2,1)S(1)}, bf16[2,64,512]{2,1,0:T(8,128)(2,1)S(1)}, u32[]{:S(2)}, u32[]{:S(2)}) collective-permute-start(bf16[2,64,512]{2,1,0:T(8,128)(2,1)S(1)} %get-tuple-element.20), channel_id=1, source_target_pairs={{0,6},{2,0},{4,2},{6,4},{1,7},{3,1},{5,3},{7,5},{8,14},{10,8},{12,... | collective-permute-start | bytes 393224 | tf_op jit(solution)/shard_map/ppermute | solution.py:8
  17.9 42.6 %collective-permute-start.1 = (bf16[2,64,512]{2,1,0:T(8,128)(2,1)S(1)}, bf16[2,64,512]{2,1,0:T(8,128)(2,1)S(1)}, u32[]{:S(2)}, u32[]{:S(2)}) collective-permute-start(bf16[2,64,512]{2,1,0:T(8,128)(2,1)S(1)} %get-tuple-element.20), channel_id=1, source_target_pairs={{0,2},{2,4},{4,6},{6,0},{1,3},{3,5},{5,7},{7,1},{8,10},{10,12},{12... | collective-permute-start | bytes 393224 | tf_op jit(solution)/shard_map/ppermute | solution.py:8
  22.7 1.7 copy-start.11
  39.6 33.5 %copy-start.8 = (pred[16384]{0:T(1024)(128)(4,1)}, pred[16384]{0:T(1024)(128)(4,1)S(1)}, u32[]{:S(2)}) copy-start(pred[16384]{0:T(1024)(128)(4,1)S(1)} %add_compare_fusion) | copy-start | bytes 49156
  42.2 18.0 %copy-start.6 = (bf16[1,2,256,256]{3,2,1,0:T(8,128)(2,1)S(1)}, bf16[1,2,256,256]{3,2,1,0:T(8,128)(2,1)}, u32[]{:S(2)}) copy-start(bf16[1,2,256,256]{3,2,1,0:T(8,128)(2,1)} %param.9) | copy-start | bytes 786436
  42.2 21.2 %copy-start.5 = (bf16[2,512,512]{2,1,0:T(8,128)(2,1)S(1)}, bf16[2,512,512]{2,1,0:T(8,128)(2,1)}, u32[]{:S(2)}) copy-start(bf16[2,512,512]{2,1,0:T(8,128)(2,1)} %get-tuple-element.21) | copy-start | bytes 3145732
  54.4 5.8 %copy-start = (bf16[512,16384]{1,0:T(8,128)(2,1)}, bf16[512,16384]{1,0:T(8,128)(2,1)S(1)}, u32[]{:S(2)}) copy-start(bf16[512,16384]{1,0:T(8,128)(2,1)S(1)} %bitcast_multiply_fusion) | copy-start | bytes 50331652
  60.5 14.2 %copy-start.2 = (bf16[512,256]{0,1:T(8,128)(2,1)}, bf16[512,256]{0,1:T(8,128)(2,1)S(1)}, u32[]{:S(2)}) copy-start(bf16[512,256]{0,1:T(8,128)(2,1)S(1)} %convolution_convert_fusion.1) | copy-start | bytes 786436
  60.5 6.4 %collective-permute-start.2 = (bf16[2,32,512]{2,1,0:T(8,128)(2,1)S(1)}, bf16[2,32,512]{2,1,0:T(8,128)(2,1)S(1)}, u32[]{:S(2)}, u32[]{:S(2)}) collective-permute-start(bf16[2,32,512]{2,1,0:T(8,128)(2,1)S(1)} %slice.337), channel_id=1, source_target_pairs={{0,2},{2,4},{4,6},{6,0},{1,3},{3,5},{5,7},{7,1},{8,10},{10,12},{12... | collective-permute-start | bytes 196616 | tf_op jit(solution)/shard_map/ppermute | solution.py:8
  60.6 6.3 %collective-permute-start.3 = (bf16[2,32,512]{2,1,0:T(8,128)(2,1)S(1)}, bf16[2,32,512]{2,1,0:T(8,128)(2,1)S(1)}, u32[]{:S(2)}, u32[]{:S(2)}) collective-permute-start(bf16[2,32,512]{2,1,0:T(8,128)(2,1)S(1)} %slice.338), channel_id=1, source_target_pairs={{0,6},{2,0},{4,2},{6,4},{1,7},{3,1},{5,3},{7,5},{8,14},{10,8},{12,... | collective-permute-start | bytes 196616 | tf_op jit(solution)/shard_map/ppermute | solution.py:8
  68.9 4.8 %collective-permute-start.5 = (bf16[256,256]{1,0:T(8,128)(2,1)S(1)}, bf16[256,256]{1,0:T(8,128)(2,1)}, u32[]{:S(2)}, u32[]{:S(2)}) collective-permute-start(bf16[256,256]{1,0:T(8,128)(2,1)S(1)} %convolution_convert_fusion.2), channel_id=1, source_target_pairs={{0,1},{2,3},{4,5},{6,7},{8,9},{10,11},{12,13},{14,15},{16,17},{18,... | collective-permute-start | bytes 393224 | tf_op jit(solution)/shard_map/ppermute | solution.py:132
  71.7 2.9 %copy-start.4 = (bf16[512,256]{0,1:T(8,128)(2,1)}, bf16[512,256]{0,1:T(8,128)(2,1)S(1)}, u32[]{:S(2)}) copy-start(bf16[512,256]{0,1:T(8,128)(2,1)S(1)} %convolution_convert_fusion) | copy-start | bytes 786436
  71.8 5.0 %collective-permute-start.4 = (bf16[512,512]{0,1:T(8,128)(2,1)S(1)}, bf16[512,512]{0,1:T(8,128)(2,1)S(1)}, u32[]{:S(2)}, u32[]{:S(2)}) collective-permute-start(bf16[512,512]{0,1:T(8,128)(2,1)S(1)} %pad_maximum_fusion.6), channel_id=1, source_target_pairs={{0,1},{2,3},{4,5},{6,7},{8,9},{10,11},{12,13},{14,15},{16,17},{18,... | collective-permute-start | bytes 1572872 | tf_op jit(solution)/shard_map/ppermute | solution.py:132
  73.7 54.1 %slice-start.1 = ((pred[16384]{0:T(1024)(128)(4,1)}), pred[11264]{0:T(1024)(128)(4,1)S(1)}, s32[]{:S(2)}) async-start(pred[16384]{0:T(1024)(128)(4,1)} %copy-done.8), calls=%async_computation.4 | async-start | bytes 22528 | tf_op jit(solution)/shard_map/slice | solution.py:153
  74.6 0.7 copy-start.7
  126.4 36.7 %collective-permute-start.6 = (bf16[2,64,5120]{2,1,0:T(8,128)(2,1)}, bf16[2,64,5120]{2,1,0:T(8,128)(2,1)}, u32[]{:S(2)}, u32[]{:S(2)}) collective-permute-start(bf16[2,64,5120]{2,1,0:T(8,128)(2,1)} %bitcast_multiply_fusion.2), channel_id=1, source_target_pairs={{0,6},{2,0},{4,2},{6,4},{1,7},{3,1},{5,3},{7,5},{8,14},{10,8},{12,... | collective-permute-start | bytes 3932168 | tf_op jit(solution)/shard_map/ppermute | solution.py:8
  127.2 30.7 %collective-permute-start.7 = (bf16[2,64,5120]{2,1,0:T(8,128)(2,1)}, bf16[2,64,5120]{2,1,0:T(8,128)(2,1)}, u32[]{:S(2)}, u32[]{:S(2)}) collective-permute-start(bf16[2,64,5120]{2,1,0:T(8,128)(2,1)} %bitcast_multiply_fusion.2), channel_id=1, source_target_pairs={{0,2},{2,4},{4,6},{6,0},{1,3},{3,5},{5,7},{7,1},{8,10},{10,12},{12... | collective-permute-start | bytes 3932168 | tf_op jit(solution)/shard_map/ppermute | solution.py:8
  141.7 0.9 copy-start.3
  159.1 15.6 %collective-permute-start.8 = (bf16[2,32,5120]{2,1,0:T(8,128)(2,1)S(1)}, bf16[2,32,5120]{2,1,0:T(8,128)(2,1)S(1)}, u32[]{:S(2)}, u32[]{:S(2)}) collective-permute-start(bf16[2,32,5120]{2,1,0:T(8,128)(2,1)S(1)} %slice.345), channel_id=1, source_target_pairs={{0,2},{2,4},{4,6},{6,0},{1,3},{3,5},{5,7},{7,1},{8,10},{10,12},{12... | collective-permute-start | bytes 1966088 | tf_op jit(solution)/shard_map/ppermute | solution.py:8
  164.2 14.5 %collective-permute-start.9 = (bf16[2,32,5120]{2,1,0:T(8,128)(2,1)S(1)}, bf16[2,32,5120]{2,1,0:T(8,128)(2,1)S(1)}, u32[]{:S(2)}, u32[]{:S(2)}) collective-permute-start(bf16[2,32,5120]{2,1,0:T(8,128)(2,1)S(1)} %slice.346), channel_id=1, source_target_pairs={{0,6},{2,0},{4,2},{6,4},{1,7},{3,1},{5,3},{7,5},{8,14},{10,8},{12,... | collective-permute-start | bytes 1966088 | tf_op jit(solution)/shard_map/ppermute | solution.py:8
  168.5 11.9 %copy-start.10 = (pred[2560]{0:T(1024)(128)(4,1)S(1)}, pred[2560]{0:T(1024)(128)(4,1)}, u32[]{:S(2)}) copy-start(pred[2560]{0:T(1024)(128)(4,1)} %get-tuple-element.40) | copy-start | bytes 7684
  180.4 6.7 %copy-start.9 = (pred[2560]{0:T(1024)(128)(4,1)S(1)}, pred[2560]{0:T(1024)(128)(4,1)}, u32[]{:S(2)}) copy-start(pred[2560]{0:T(1024)(128)(4,1)} %get-tuple-element.41) | copy-start | bytes 7684
  184.1 16.9 %collective-permute-start.10 = (bf16[2,32,2560]{2,1,0:T(8,128)(2,1)S(1)}, bf16[2,32,2560]{2,1,0:T(8,128)(2,1)S(1)}, u32[]{:S(2)}, u32[]{:S(2)}) collective-permute-start(bf16[2,32,2560]{2,1,0:T(8,128)(2,1)S(1)} %get-tuple-element.32), channel_id=1, source_target_pairs={{0,8},{8,16},{16,24},{24,0},{32,40},{40,48},{48,56},{56,32},{64,72... | collective-permute-start | bytes 983048 | tf_op jit(solution)/shard_map/ppermute | solution.py:26
  185.9 16.2 %collective-permute-start.12 = (bf16[2,32,2560]{2,1,0:T(8,128)(2,1)S(1)}, bf16[2,32,2560]{2,1,0:T(8,128)(2,1)S(1)}, u32[]{:S(2)}, u32[]{:S(2)}) collective-permute-start(bf16[2,32,2560]{2,1,0:T(8,128)(2,1)S(1)} %get-tuple-element.33), channel_id=1, source_target_pairs={{0,24},{8,0},{16,8},{24,16},{32,56},{40,32},{48,40},{56,48},{64,88... | collective-permute-start | bytes 983048 | tf_op jit(solution)/shard_map/ppermute | solution.py:26
  187.1 6.5 %copy-start.1 = (bf16[2,64,5120]{2,1,0:T(8,128)(2,1)S(1)}, bf16[2,64,5120]{2,1,0:T(8,128)(2,1)}, u32[]{:S(2)}) copy-start(bf16[2,64,5120]{2,1,0:T(8,128)(2,1)} %bitcast_multiply_fusion.2) | copy-start | bytes 3932164
  190.7 16.0 %collective-permute-start.18 = (bf16[2,32,2560]{2,1,0:T(8,128)(2,1)S(1)}, bf16[2,32,2560]{2,1,0:T(8,128)(2,1)S(1)}, u32[]{:S(2)}, u32[]{:S(2)}) collective-permute-start(bf16[2,32,2560]{2,1,0:T(8,128)(2,1)S(1)} %get-tuple-element.34), channel_id=1, source_target_pairs={{0,32},{8,40},{16,48},{24,56},{32,64},{40,72},{48,80},{56,88},{64,... | collective-permute-start | bytes 983048 | tf_op jit(solution)/shard_map/ppermute | solution.py:26
  192.3 14.4 %collective-permute-start.20 = (bf16[2,32,2560]{2,1,0:T(8,128)(2,1)S(1)}, bf16[2,32,2560]{2,1,0:T(8,128)(2,1)S(1)}, u32[]{:S(2)}, u32[]{:S(2)}) collective-permute-start(bf16[2,32,2560]{2,1,0:T(8,128)(2,1)S(1)} %get-tuple-element.35), channel_id=1, source_target_pairs={{0,96},{8,104},{16,112},{24,120},{32,0},{40,8},{48,16},{56,24},{64... | collective-permute-start | bytes 983048 | tf_op jit(solution)/shard_map/ppermute | solution.py:26
  201.1 23.9 %collective-permute-start.11 = (bf16[4,32,2560]{2,1,0:T(8,128)(2,1)S(1)}, bf16[4,32,2560]{2,1,0:T(8,128)(2,1)S(1)}, u32[]{:S(2)}, u32[]{:S(2)}) collective-permute-start(bf16[4,32,2560]{2,1,0:T(8,128)(2,1)S(1)} %pad_maximum_fusion), channel_id=1, source_target_pairs={{0,8},{8,16},{16,24},{24,0},{32,40},{40,48},{48,56},{56,32},{64,72... | collective-permute-start | bytes 1966088 | tf_op jit(solution)/shard_map/ppermute | solution.py:26
  202.3 22.8 %collective-permute-start.13 = (bf16[4,32,2560]{2,1,0:T(8,128)(2,1)S(1)}, bf16[4,32,2560]{2,1,0:T(8,128)(2,1)S(1)}, u32[]{:S(2)}, u32[]{:S(2)}) collective-permute-start(bf16[4,32,2560]{2,1,0:T(8,128)(2,1)S(1)} %pad_maximum_fusion.1), channel_id=1, source_target_pairs={{0,24},{8,0},{16,8},{24,16},{32,56},{40,32},{48,40},{56,48},{64,88... | collective-permute-start | bytes 1966088 | tf_op jit(solution)/shard_map/ppermute | solution.py:26
  206.9 21.1 %collective-permute-start.19 = (bf16[4,32,2560]{2,1,0:T(8,128)(2,1)S(1)}, bf16[4,32,2560]{2,1,0:T(8,128)(2,1)S(1)}, u32[]{:S(2)}, u32[]{:S(2)}) collective-permute-start(bf16[4,32,2560]{2,1,0:T(8,128)(2,1)S(1)} %pad_maximum_fusion.2), channel_id=1, source_target_pairs={{0,32},{8,40},{16,48},{24,56},{32,64},{40,72},{48,80},{56,88},{64,... | collective-permute-start | bytes 1966088 | tf_op jit(solution)/shard_map/ppermute | solution.py:26
  207.1 21.0 %collective-permute-start.21 = (bf16[4,32,2560]{2,1,0:T(8,128)(2,1)S(1)}, bf16[4,32,2560]{2,1,0:T(8,128)(2,1)S(1)}, u32[]{:S(2)}, u32[]{:S(2)}) collective-permute-start(bf16[4,32,2560]{2,1,0:T(8,128)(2,1)S(1)} %pad_maximum_fusion.3), channel_id=1, source_target_pairs={{0,96},{8,104},{16,112},{24,120},{32,0},{40,8},{48,16},{56,24},{64... | collective-permute-start | bytes 1966088 | tf_op jit(solution)/shard_map/ppermute | solution.py:26
  225.3 5.9 %collective-permute-start.14 = (bf16[16,2560]{1,0:T(8,128)(2,1)S(1)}, bf16[16,2560]{1,0:T(8,128)(2,1)S(1)}, u32[]{:S(2)}, u32[]{:S(2)}) collective-permute-start(bf16[16,2560]{1,0:T(8,128)(2,1)S(1)} %get-tuple-element.36), channel_id=1, source_target_pairs={{0,32},{8,40},{16,48},{24,56},{32,64},{40,72},{48,80},{56,88},{64,... | collective-permute-start | bytes 245768 | tf_op jit(solution)/shard_map/ppermute | solution.py:26
  225.6 5.6 %collective-permute-start.16 = (bf16[16,2560]{1,0:T(8,128)(2,1)S(1)}, bf16[16,2560]{1,0:T(8,128)(2,1)S(1)}, u32[]{:S(2)}, u32[]{:S(2)}) collective-permute-start(bf16[16,2560]{1,0:T(8,128)(2,1)S(1)} %get-tuple-element.37), channel_id=1, source_target_pairs={{0,96},{8,104},{16,112},{24,120},{32,0},{40,8},{48,16},{56,24},{64... | collective-permute-start | bytes 245768 | tf_op jit(solution)/shard_map/ppermute | solution.py:26
  228.5 6.6 %collective-permute-start.22 = (bf16[16,2560]{1,0:T(8,128)(2,1)S(1)}, bf16[16,2560]{1,0:T(8,128)(2,1)S(1)}, u32[]{:S(2)}, u32[]{:S(2)}) collective-permute-start(bf16[16,2560]{1,0:T(8,128)(2,1)S(1)} %get-tuple-element.38), channel_id=1, source_target_pairs={{0,8},{8,16},{16,24},{24,0},{32,40},{40,48},{48,56},{56,32},{64,72... | collective-permute-start | bytes 245768 | tf_op jit(solution)/shard_map/ppermute | solution.py:26
  228.8 6.3 %collective-permute-start.24 = (bf16[16,2560]{1,0:T(8,128)(2,1)S(1)}, bf16[16,2560]{1,0:T(8,128)(2,1)S(1)}, u32[]{:S(2)}, u32[]{:S(2)}) collective-permute-start(bf16[16,2560]{1,0:T(8,128)(2,1)S(1)} %get-tuple-element.39), channel_id=1, source_target_pairs={{0,24},{8,0},{16,8},{24,16},{32,56},{40,32},{48,40},{56,48},{64,88... | collective-permute-start | bytes 245768 | tf_op jit(solution)/shard_map/ppermute | solution.py:26
  231.3 9.3 %collective-permute-start.15 = (bf16[32,2560]{1,0:T(8,128)(2,1)S(1)}, bf16[32,2560]{1,0:T(8,128)(2,1)S(1)}, u32[]{:S(2)}, u32[]{:S(2)}) collective-permute-start(bf16[32,2560]{1,0:T(8,128)(2,1)S(1)} %pad_maximum_fusion.10), channel_id=1, source_target_pairs={{0,32},{8,40},{16,48},{24,56},{32,64},{40,72},{48,80},{56,88},{64,... | collective-permute-start | bytes 491528 | tf_op jit(solution)/shard_map/ppermute | solution.py:26
  231.4 9.5 %collective-permute-start.17 = (bf16[32,2560]{1,0:T(8,128)(2,1)S(1)}, bf16[32,2560]{1,0:T(8,128)(2,1)S(1)}, u32[]{:S(2)}, u32[]{:S(2)}) collective-permute-start(bf16[32,2560]{1,0:T(8,128)(2,1)S(1)} %pad_maximum_fusion.11), channel_id=1, source_target_pairs={{0,96},{8,104},{16,112},{24,120},{32,0},{40,8},{48,16},{56,24},{64... | collective-permute-start | bytes 491528 | tf_op jit(solution)/shard_map/ppermute | solution.py:26
  235.1 9.6 %collective-permute-start.23 = (bf16[32,2560]{1,0:T(8,128)(2,1)S(1)}, bf16[32,2560]{1,0:T(8,128)(2,1)S(1)}, u32[]{:S(2)}, u32[]{:S(2)}) collective-permute-start(bf16[32,2560]{1,0:T(8,128)(2,1)S(1)} %pad_maximum_fusion.12), channel_id=1, source_target_pairs={{0,8},{8,16},{16,24},{24,0},{32,40},{40,48},{48,56},{56,32},{64,72... | collective-permute-start | bytes 491528 | tf_op jit(solution)/shard_map/ppermute | solution.py:26
  235.3 9.4 %collective-permute-start.25 = (bf16[32,2560]{1,0:T(8,128)(2,1)S(1)}, bf16[32,2560]{1,0:T(8,128)(2,1)S(1)}, u32[]{:S(2)}, u32[]{:S(2)}) collective-permute-start(bf16[32,2560]{1,0:T(8,128)(2,1)S(1)} %pad_maximum_fusion.13), channel_id=1, source_target_pairs={{0,24},{8,0},{16,8},{24,16},{32,56},{40,32},{48,40},{56,48},{64,88... | collective-permute-start | bytes 491528 | tf_op jit(solution)/shard_map/ppermute | solution.py:26
Sparse Core Ops, SparseCore 0:
  11.8 114.5 all-gather.1
  141.8 106.9 reduce-scatter.1
where the time goes:
time: 259 us; the launch traced here: 258 us
  waiting for transfers between devices  106 us (41%)
  local copies, waits for them, and re-layouts  40.7 us (16%)
  starting transfers between devices  37.6 us (15%)
  other arithmetic  29.5 us (11%)
  matrix products  29.4 us (11%)
  between operations  14.8 us (6%)
    all_gather x1, waiting for transfers between devices, on_device(): gathered = lax.all_gather(first_cols, 'prow', axis=1, tiled=True)  44.8 us
    ppermute x16, waiting for transfers between devices, grid_shift(): return lax.ppermute(value, axis, pairs)  29.7 us
    unnamed x44, local copies, waits for them, and re-layouts  26.8 us
    ppermute x8, waiting for transfers between devices, ring(): lax.ppermute(value, axis, [(i, (i + step) % size) for i in range(size)])  26.3 us
    ppermute x16, starting transfers between devices, grid_shift(): return lax.ppermute(value, axis, pairs)  23.2 us
    dot_general x1, matrix products, on_device(): jnp.dot(multipliers, gathered.reshape(2 * block_size, half), preferred_el...  13.9 us
    mul x1, other arithmetic, on_device(): front[0]  12.2 us
    ppermute x8, starting transfers between devices, ring(): lax.ppermute(value, axis, [(i, (i + step) % size) for i in range(size)])  11.7 us
  transfers between devices with their start and end apart: 28, of which 14 were waited for; matrix products, arithmetic and copies ran while one was open for 33% of the time, Pallas kernels for 0%

commit v1 on v0

--- a/solution.py
+++ b/solution.py
@@ -2,6 +2,11 @@
 import jax.numpy as jnp
 from jax import lax
 from jax.sharding import PartitionSpec as P
+
+
+def gather_over(x, axis, dim):
+    repeated = jnp.stack([x] * lax.axis_size(axis))
+    return jnp.concatenate(lax.all_to_all(repeated, axis, 0, 0), axis=dim)
 
 
 def ring(value, axis, size, step):
@@ -105,7 +110,7 @@
     assert n_prow == 4
     half = col_count * 11 // 16 // block_size * block_size
     first_cols = mask_pivots(0, half)
-    gathered = lax.all_gather(first_cols, "prow", axis=1, tiled=True)
+    gathered = gather_over(first_cols, "prow", 1)
     later_cols, gathered = lax.optimization_barrier((mask_pivots(half, col_count), gathered))
     panel = jnp.roll(
         gather_relative(first_cols[:, :, :panel_width], "prow", n_prow), row_offset, axis=1

time: 259 us -> 315 us (1.22)
  waiting for transfers between devices: 106 us -> 140 us
  local copies, waits for them, and re-layouts: 40.7 us -> 52.8 us
  starting transfers between devices: 37.6 us -> 43.6 us
    ppermute x8, waiting for transfers between devices: 26.3 us -> 104 us  [ring(): lax.ppermute(value, axis, [(i, (i + step) % size) for i in range(size)])]
    all_gather x1 -> x0, waiting for transfers between devices: 44.8 us -> none  [on_device(): gathered = lax.all_gather(first_cols, 'prow', axis=1, tiled=True)]
    all_to_all x0 -> x1, local copies, waits for them, and re-layouts: none -> 9.97 us  [gather_over(): return jnp.concatenate(lax.all_to_all(repeated, axis, 0, 0), axis=dim)]
    all_to_all x0 -> x1, starting transfers between devices: none -> 6.41 us  [gather_over(): return jnp.concatenate(lax.all_to_all(repeated, axis, 0, 0), axis=dim)]
    another operation x0 -> x1, local copies, waits for them, and re-layouts: none -> 5.59 us  [gather_over(): repeated = jnp.stack([x] * lax.axis_size(axis))]
    slice x0 -> x1, other arithmetic: none -> 3.94 us  [mask_pivots(): pivots[0, :, :, lo:hi]]
    mul x2 -> x1, other arithmetic: 6.1 us -> 2.48 us  [mask_pivots(): pivots[0, :, :, lo:hi]]
    unnamed x44 -> x46, local copies, waits for them, and re-layouts: 26.8 us -> 25 us
  transfers between devices with their start and end apart: 28 -> 28, of which waited for: 14 -> 14; matrix products, arithmetic and copies ran while one was open for 33% -> 29% of each run, Pallas kernels for 0% -> 0%
where the time goes in v1:
time: 315 us; the launch traced here: 314 us
  waiting for transfers between devices  140 us (44%)
  local copies, waits for them, and re-layouts  52.8 us (17%)
  starting transfers between devices  43.6 us (14%)
  matrix products  32.4 us (10%)
  other arithmetic  30.3 us (10%)
  between operations  14.9 us (5%)
    ppermute x8, waiting for transfers between devices, ring(): lax.ppermute(value, axis, [(i, (i + step) % size) for i in range(size)])  104 us
    ppermute x16, waiting for transfers between devices, grid_shift(): return lax.ppermute(value, axis, pairs)  28.8 us
    unnamed x46, local copies, waits for them, and re-layouts  25 us
    ppermute x16, starting transfers between devices, grid_shift(): return lax.ppermute(value, axis, pairs)  22.9 us
    dot_general x1, matrix products, on_device(): jnp.dot(multipliers, gathered.reshape(2 * block_size, half), preferred_el...  15.9 us
    mul x1, other arithmetic, on_device(): front[0]  12.1 us
    ppermute x8, starting transfers between devices, ring(): lax.ppermute(value, axis, [(i, (i + step) % size) for i in range(size)])  11.7 us
    all_to_all x1, local copies, waits for them, and re-layouts, gather_over(): return jnp.concatenate(lax.all_to_all(repeated, axis, 0, 0), axis=dim)  9.97 us
  transfers between devices with their start and end apart: 28, of which 14 were waited for; matrix products, arithmetic and copies ran while one was open for 29% of the time, Pallas kernels for 0%

profile of v1, /device:TPU:1, one launch (start us, length us, event | category | flops | bytes accessed | tf_op | source)
XLA Modules:
  0.0 313.6 jit_solution(9358122784894011656)
XLA Ops:
  8.0 3.9 %fusion.61 = (bf16[1,2,64,11264]{3,2,1,0:T(8,128)(2,1)}, bf16[2,64,11264]{2,1,0:T(8,128)(2,1)S(1)}, bf16[2,64,11264]{2,1,0:T(8,128)(2,1)S(1)}) fusion(bf16[1,2,64,16384]{3,2,1,0:T(8,128)(2,1)} %param.8, bf16[2,11264]{1,0:T(2,128)(2,1)S(1)} %bitcast.184), kind=kLoop, calls=%fused_computation.153 | loop fusion | flops 1441792 | bytes 11579392 | tf_op jit(solution)/shard_map/slice | solution.py:98
  11.9 0.7 constant_dynamic-update-slice_fusion.9
  12.6 4.6 %collective-permute-start = (bf16[2,64,512]{2,1,0:T(8,128)(2,1)S(1)}, bf16[2,64,512]{2,1,0:T(8,128)(2,1)S(1)}, u32[]{:S(2)}, u32[]{:S(2)}) collective-permute-start(bf16[2,64,512]{2,1,0:T(8,128)(2,1)S(1)} %get-tuple-element.18), channel_id=1, source_target_pairs={{0,6},{2,0},{4,2},{6,4},{1,7},{3,1},{5,3},{7,5},{8,14},{10,8},{12,... | collective-permute-start | bytes 393224 | tf_op jit(solution)/shard_map/ppermute | solution.py:13
  17.2 5.6 %stack.3 = bf16[4,2,64,11264]{3,2,1,0:T(8,128)(2,1)} broadcast(bf16[2,64,11264]{2,1,0:T(8,128)(2,1)S(1)} %get-tuple-element.27), dimensions={1,2,3} | broadcast | bytes 14417920 | tf_op jit(solution)/shard_map/stack | solution.py:8
  22.8 6.4 %all-to-all-start = ((bf16[4,2,64,11264]{3,2,1,0:T(8,128)(2,1)}), bf16[4,2,64,11264]{3,2,1,0:T(8,128)(2,1)}, u32[]{:S(2)}, u32[]{:S(2)}) async-start(bf16[4,2,64,11264]{3,2,1,0:T(8,128)(2,1)} %stack.3), calls=%async_computation | async-start | bytes 23068672 | tf_op jit(solution)/shard_map/all_to_all | solution.py:9
  29.6 3.0 reshape_squeeze.14
  32.6 1.7 fusion.6
  34.3 1.6 copy.24
  36.0 2.7 mul.53
  38.7 12.4 %copy.22 = bf16[64,8,64,256]{3,1,2,0:T(8,128)(2,1)} copy(bf16[64,8,64,256]{3,2,1,0:T(8,128)(2,1)S(1)} %bitcast.168) | data formatting | bytes 33554432
  51.3 2.5 bitcast_multiply_fusion.1
  53.7 12.1 %bitcast_multiply_fusion = bf16[512,16384]{1,0:T(8,128)(2,1)S(1)} fusion(bf16[512,16384]{1,0:T(8,128)(2,1)} %bitcast.167, bf16[1,512,16384]{2,1,0:T(8,128)(2,1)} %param.7), kind=kLoop, calls=%fused_computation.1 | loop fusion | flops 8388608 | bytes 50331648 | tf_op jit(solution)/shard_map/mul | solution.py:92
  65.8 5.8 %copy-done = bf16[512,16384]{1,0:T(8,128)(2,1)} copy-done((bf16[512,16384]{1,0:T(8,128)(2,1)}, bf16[512,16384]{1,0:T(8,128)(2,1)S(1)}, u32[]{:S(2)}) %copy-start) | copy-done | bytes 16777240
  71.9 1.4 collective-permute-start.2
  73.3 1.4 collective-permute-start.3
  74.7 79.0 %collective-permute-done.2 = bf16[2,32,512]{2,1,0:T(8,128)(2,1)S(1)} collective-permute-done((bf16[2,32,512]{2,1,0:T(8,128)(2,1)S(1)}, bf16[2,32,512]{2,1,0:T(8,128)(2,1)S(1)}, u32[]{:S(2)}, u32[]{:S(2)}) %collective-permute-start.2) | collective-permute-done | bytes 65568 | tf_op jit(solution)/shard_map/ppermute | solution.py:13
  153.8 2.0 collective-permute-done.3
  155.9 0.7 dynamic-slice_bitcast_fusion.4
  156.8 1.3 collective-permute-start.5
  158.1 1.5 convolution_convert_fusion
  159.7 1.3 collective-permute-start.4
  162.0 0.9 broadcast_select_fusion.1
  163.6 2.4 collective-permute-done.4
  166.0 1.2 broadcast_select_fusion
  167.1 0.7 slice.342
  167.8 1.0 copy.17
  168.8 1.9 subtract_convert_fusion
  170.7 10.0 %copy.13 = bf16[4,2,64,11264]{3,2,0,1:T(8,128)(2,1)} copy(bf16[4,2,64,11264]{3,2,1,0:T(8,128)(2,1)} %all-to-all-done) | data formatting | bytes 23068672 | tf_op jit(solution)/shard_map/all_to_all | solution.py:9
  181.3 0.8 collective-permute-start.7
  182.2 15.9 %select_convert_fusion = bf16[512,11264]{1,0:T(8,128)(2,1)} fusion(bf16[512,11264]{1,0:T(8,128)(2,1)} %bitcast.169, bf16[512,16384]{1,0:T(8,128)(2,1)} %copy-done, pred[11264]{0:T(1024)(128)(4,1)S(1)} %slice-done, bf16[512,256]{0,1:T(8,128)(2,1)S(1)} %copy-done.3, bf16[512,256]{0,1:T(8,128)(2,1)S(1)} %copy-done.7), kind=kOutput, calls=%fused_computation | convolution fusion | flops 5929697280 | bytes 35138560 | tf_op jit(solution)/shard_map/dot_general | solution.py:155
  198.1 1.4 fusion.25
  199.5 1.4 constant_dynamic-update-slice_fusion.14
  200.9 11.9 %collective-permute-done.7 = bf16[2,64,5120]{2,1,0:T(8,128)(2,1)} collective-permute-done((bf16[2,64,5120]{2,1,0:T(8,128)(2,1)}, bf16[2,64,5120]{2,1,0:T(8,128)(2,1)}, u32[]{:S(2)}, u32[]{:S(2)}) %collective-permute-start.7) | collective-permute-done | bytes 1310752 | tf_op jit(solution)/shard_map/ppermute | solution.py:13
  212.8 1.1 slice.346
  214.0 3.9 %fusion = bf16[64,11264]{1,0:T(8,128)(2,1)S(1)} fusion(f32[64,11264]{1,0:T(8,128)S(1)} %bitcast.172, bf16[64,256]{1,0:T(8,128)(2,1)S(1)} %constant_dynamic-slice_fusion, bf16[2,256,11264]{2,1,0:T(8,128)(2,1)} %bitcast.170), kind=kOutput, calls=%fused_computation.3 | convolution fusion | flops 370540544 | bytes 10125312 | tf_op jit(solution)/shard_map/dot_general | solution.py:170
  217.9 1.1 slice.347
  219.0 2.7 collective-permute-start.9
  221.8 1.5 constant_dynamic-update-slice_fusion.13
  223.3 7.0 %collective-permute-done.8 = bf16[2,32,5120]{2,1,0:T(8,128)(2,1)S(1)} collective-permute-done((bf16[2,32,5120]{2,1,0:T(8,128)(2,1)S(1)}, bf16[2,32,5120]{2,1,0:T(8,128)(2,1)S(1)}, u32[]{:S(2)}, u32[]{:S(2)}) %collective-permute-start.8) | collective-permute-done | bytes 655392 | tf_op jit(solution)/shard_map/ppermute | solution.py:13
  230.3 3.9 %collective-permute-done.9 = bf16[2,32,5120]{2,1,0:T(8,128)(2,1)S(1)} collective-permute-done((bf16[2,32,5120]{2,1,0:T(8,128)(2,1)S(1)}, bf16[2,32,5120]{2,1,0:T(8,128)(2,1)S(1)}, u32[]{:S(2)}, u32[]{:S(2)}) %collective-permute-start.9) | collective-permute-done | bytes 655392 | tf_op jit(solution)/shard_map/ppermute | solution.py:13
  234.3 1.5 constant_dynamic-update-slice_fusion.10
  235.9 3.6 %subtract_select_fusion.1 = f32[512,2560]{1,0:T(8,128)S(1)} fusion(bf16[512,5120]{1,0:T(8,128)(2,1)S(1)} %bitcast.181, bf16[512,16384]{1,0:T(8,128)(2,1)} %copy-done, pred[2560]{0:T(1024)(128)(4,1)S(1)} %copy-done.11, bf16[512,256]{0,1:T(8,128)(2,1)S(1)} %get-tuple-element.48, bf16[512,256]{0,1:T(8,128)(2,1)S(1)} %get-tuple-element.49), kind=kOutput, calls=%fused_computation.9 | convolution fusion | flops 1347158016 | bytes 11013120 | tf_op jit(solution)/shard_map/dot_general | solution.py:188
  239.6 1.0 collective-permute-start.10
  240.6 1.7 collective-permute-start.12
  242.3 3.4 %subtract_select_fusion = f32[512,2560]{1,0:T(8,128)S(1)} fusion(bf16[512,5120]{1,0:T(8,128)(2,1)S(1)} %bitcast.182, bf16[512,16384]{1,0:T(8,128)(2,1)} %copy-done, pred[2560]{0:T(1024)(128)(4,1)S(1)} %copy-done.10, bf16[512,256]{0,1:T(8,128)(2,1)S(1)} %get-tuple-element.48, bf16[512,256]{0,1:T(8,128)(2,1)S(1)} %get-tuple-element.49), kind=kOutput, calls=%fused_computation.8 | convolution fusion | flops 1347158016 | bytes 11013120 | tf_op jit(solution)/shard_map/dot_general | solution.py:188
  245.9 1.1 collective-permute-start.18
  247.0 1.6 collective-permute-start.20
  248.6 1.8 fusion.1
  250.7 1.5 maximum_bitcast_fusion.1
  252.3 4.3 %collective-permute-done.10 = bf16[2,32,2560]{2,1,0:T(8,128)(2,1)S(1)} collective-permute-done((bf16[2,32,2560]{2,1,0:T(8,128)(2,1)S(1)}, bf16[2,32,2560]{2,1,0:T(8,128)(2,1)S(1)}, u32[]{:S(2)}, u32[]{:S(2)}) %collective-permute-start.10) | collective-permute-done | bytes 327712 | tf_op jit(solution)/shard_map/ppermute | solution.py:31
  257.1 2.7 collective-permute-start.13
  259.9 0.9 collective-permute-done.18
  260.9 0.9 collective-permute-start.19
  261.9 1.9 collective-permute-start.21
  263.8 16.9 %collective-permute-done.11 = bf16[4,32,2560]{2,1,0:T(8,128)(2,1)S(1)} collective-permute-done((bf16[4,32,2560]{2,1,0:T(8,128)(2,1)S(1)}, bf16[4,32,2560]{2,1,0:T(8,128)(2,1)S(1)}, u32[]{:S(2)}, u32[]{:S(2)}) %collective-permute-start.11) | collective-permute-done | bytes 655392 | tf_op jit(solution)/shard_map/ppermute | solution.py:31
  281.0 2.7 collective-permute-start.16
  284.4 2.4 collective-permute-start.24
  287.0 3.2 %collective-permute-start.17 = (bf16[32,2560]{1,0:T(8,128)(2,1)S(1)}, bf16[32,2560]{1,0:T(8,128)(2,1)S(1)}, u32[]{:S(2)}, u32[]{:S(2)}) collective-permute-start(bf16[32,2560]{1,0:T(8,128)(2,1)S(1)} %pad_maximum_fusion.11), channel_id=1, source_target_pairs={{0,96},{8,104},{16,112},{24,120},{32,0},{40,8},{48,16},{56,24},{64... | collective-permute-start | bytes 491528 | tf_op jit(solution)/shard_map/ppermute | solution.py:31
  290.8 2.7 collective-permute-start.25
  293.5 3.2 %collective-permute-done.15 = bf16[32,2560]{1,0:T(8,128)(2,1)S(1)} collective-permute-done((bf16[32,2560]{1,0:T(8,128)(2,1)S(1)}, bf16[32,2560]{1,0:T(8,128)(2,1)S(1)}, u32[]{:S(2)}, u32[]{:S(2)}) %collective-permute-start.15) | collective-permute-done | bytes 163872 | tf_op jit(solution)/shard_map/ppermute | solution.py:31
  296.7 3.2 %collective-permute-done.23 = bf16[32,2560]{1,0:T(8,128)(2,1)S(1)} collective-permute-done((bf16[32,2560]{1,0:T(8,128)(2,1)S(1)}, bf16[32,2560]{1,0:T(8,128)(2,1)S(1)}, u32[]{:S(2)}, u32[]{:S(2)}) %collective-permute-start.23) | collective-permute-done | bytes 163872 | tf_op jit(solution)/shard_map/ppermute | solution.py:31
  300.0 4.1 %reduce-scatter.2.cloned.1.call-done = bf16[32,11264]{1,0:T(8,128)(2,1)} async-done(((bf16[512,11264]{1,0:T(8,128)(2,1)}), bf16[32,11264]{1,0:T(8,128)(2,1)}) %reduce-scatter.2.cloned.1.call-update) | async-done | bytes 720912 | tf_op jit(solution)/shard_map/reduce_scatter | solution.py:161
  304.1 1.2 convert_element_type.165
  305.3 1.5 maximum_bitcast_fusion
  (113 shorter events, 7.2 us)
Async XLA Ops:
  12.6 60.7 %collective-permute-start = (bf16[2,64,512]{2,1,0:T(8,128)(2,1)S(1)}, bf16[2,64,512]{2,1,0:T(8,128)(2,1)S(1)}, u32[]{:S(2)}, u32[]{:S(2)}) collective-permute-start(bf16[2,64,512]{2,1,0:T(8,128)(2,1)S(1)} %get-tuple-element.18), channel_id=1, source_target_pairs={{0,6},{2,0},{4,2},{6,4},{1,7},{3,1},{5,3},{7,5},{8,14},{10,8},{12,... | collective-permute-start | bytes 393224 | tf_op jit(solution)/shard_map/ppermute | solution.py:13
  17.2 54.7 %collective-permute-start.1 = (bf16[2,64,512]{2,1,0:T(8,128)(2,1)S(1)}, bf16[2,64,512]{2,1,0:T(8,128)(2,1)S(1)}, u32[]{:S(2)}, u32[]{:S(2)}) collective-permute-start(bf16[2,64,512]{2,1,0:T(8,128)(2,1)S(1)} %get-tuple-element.18), channel_id=1, source_target_pairs={{0,2},{2,4},{4,6},{6,0},{1,3},{3,5},{5,7},{7,1},{8,10},{10,12},{12... | collective-permute-start | bytes 393224 | tf_op jit(solution)/shard_map/ppermute | solution.py:13
  22.8 6.8 %copy-start.1 = (bf16[1,2,64,11264]{3,2,1,0:T(8,128)(2,1)S(1)}, bf16[1,2,64,11264]{3,2,1,0:T(8,128)(2,1)}, u32[]{:S(2)}) copy-start(bf16[1,2,64,11264]{3,2,1,0:T(8,128)(2,1)} %get-tuple-element.25) | copy-start | bytes 8650756
  22.8 147.9 %all-to-all-start = ((bf16[4,2,64,11264]{3,2,1,0:T(8,128)(2,1)}), bf16[4,2,64,11264]{3,2,1,0:T(8,128)(2,1)}, u32[]{:S(2)}, u32[]{:S(2)}) async-start(bf16[4,2,64,11264]{3,2,1,0:T(8,128)(2,1)} %stack.3), calls=%async_computation | async-start | bytes 23068672 | tf_op jit(solution)/shard_map/all_to_all | solution.py:9
  29.2 274.9 %reduce-scatter.2.cloned.1.call-start = ((), (), s32[]{:S(2)}) async-start(), calls=%async_computation.2 | async-start | bytes 12255232 | tf_op jit(solution)/shard_map/reduce_scatter | solution.py:161
  34.3 1.7 copy-start.12
  51.2 109.8 %copy-start.9 = (pred[16384]{0:T(1024)(128)(4,1)}, pred[16384]{0:T(1024)(128)(4,1)S(1)}, u32[]{:S(2)}) copy-start(pred[16384]{0:T(1024)(128)(4,1)S(1)} %add_compare_fusion) | copy-start | bytes 49156
  53.7 17.9 %copy-start.6 = (bf16[1,2,256,256]{3,2,1,0:T(8,128)(2,1)S(1)}, bf16[1,2,256,256]{3,2,1,0:T(8,128)(2,1)}, u32[]{:S(2)}) copy-start(bf16[1,2,256,256]{3,2,1,0:T(8,128)(2,1)} %param.9) | copy-start | bytes 786436
  53.7 21.0 %copy-start.5 = (bf16[2,512,512]{2,1,0:T(8,128)(2,1)S(1)}, bf16[2,512,512]{2,1,0:T(8,128)(2,1)}, u32[]{:S(2)}) copy-start(bf16[2,512,512]{2,1,0:T(8,128)(2,1)} %get-tuple-element.17) | copy-start | bytes 3145732
  65.8 5.8 %copy-start = (bf16[512,16384]{1,0:T(8,128)(2,1)}, bf16[512,16384]{1,0:T(8,128)(2,1)S(1)}, u32[]{:S(2)}) copy-start(bf16[512,16384]{1,0:T(8,128)(2,1)S(1)} %bitcast_multiply_fusion) | copy-start | bytes 50331652
  71.9 91.1 %copy-start.2 = (bf16[512,256]{0,1:T(8,128)(2,1)}, bf16[512,256]{0,1:T(8,128)(2,1)S(1)}, u32[]{:S(2)}) copy-start(bf16[512,256]{0,1:T(8,128)(2,1)S(1)} %convolution_convert_fusion.1) | copy-start | bytes 786436
  71.9 81.9 %collective-permute-start.2 = (bf16[2,32,512]{2,1,0:T(8,128)(2,1)S(1)}, bf16[2,32,512]{2,1,0:T(8,128)(2,1)S(1)}, u32[]{:S(2)}, u32[]{:S(2)}) collective-permute-start(bf16[2,32,512]{2,1,0:T(8,128)(2,1)S(1)} %slice.338), channel_id=1, source_target_pairs={{0,2},{2,4},{4,6},{6,0},{1,3},{3,5},{5,7},{7,1},{8,10},{10,12},{12... | collective-permute-start | bytes 196616 | tf_op jit(solution)/shard_map/ppermute | solution.py:13
  73.3 82.4 %collective-permute-start.3 = (bf16[2,32,512]{2,1,0:T(8,128)(2,1)S(1)}, bf16[2,32,512]{2,1,0:T(8,128)(2,1)S(1)}, u32[]{:S(2)}, u32[]{:S(2)}) collective-permute-start(bf16[2,32,512]{2,1,0:T(8,128)(2,1)S(1)} %slice.339), channel_id=1, source_target_pairs={{0,6},{2,0},{4,2},{6,4},{1,7},{3,1},{5,3},{7,5},{8,14},{10,8},{12,... | collective-permute-start | bytes 196616 | tf_op jit(solution)/shard_map/ppermute | solution.py:13
  156.8 5.2 %collective-permute-start.5 = (bf16[256,256]{1,0:T(8,128)(2,1)S(1)}, bf16[256,256]{1,0:T(8,128)(2,1)}, u32[]{:S(2)}, u32[]{:S(2)}) collective-permute-start(bf16[256,256]{1,0:T(8,128)(2,1)S(1)} %convolution_convert_fusion.2), channel_id=1, source_target_pairs={{0,1},{2,3},{4,5},{6,7},{8,9},{10,11},{12,13},{14,15},{16,17},{18,... | collective-permute-start | bytes 393224 | tf_op jit(solution)/shard_map/ppermute | solution.py:137
  159.6 3.3 %copy-start.4 = (bf16[512,256]{0,1:T(8,128)(2,1)}, bf16[512,256]{0,1:T(8,128)(2,1)S(1)}, u32[]{:S(2)}) copy-start(bf16[512,256]{0,1:T(8,128)(2,1)S(1)} %convolution_convert_fusion) | copy-start | bytes 786436
  159.7 6.3 %collective-permute-start.4 = (bf16[512,512]{0,1:T(8,128)(2,1)S(1)}, bf16[512,512]{0,1:T(8,128)(2,1)S(1)}, u32[]{:S(2)}, u32[]{:S(2)}) collective-permute-start(bf16[512,512]{0,1:T(8,128)(2,1)S(1)} %pad_maximum_fusion.6), channel_id=1, source_target_pairs={{0,1},{2,3},{4,5},{6,7},{8,9},{10,11},{12,13},{14,15},{16,17},{18,... | collective-permute-start | bytes 1572872 | tf_op jit(solution)/shard_map/ppermute | solution.py:137
  162.9 0.6 copy-start.8
  170.7 11.4 %copy-start.3 = (bf16[512,256]{0,1:T(8,128)(2,1)S(1)}, bf16[512,256]{0,1:T(8,128)(2,1)}, u32[]{:S(2)}) copy-start(bf16[512,256]{0,1:T(8,128)(2,1)} %slice.342) | copy-start | bytes 786436
  170.7 11.4 %copy-start.7 = (bf16[512,256]{0,1:T(8,128)(2,1)S(1)}, bf16[512,256]{0,1:T(8,128)(2,1)}, u32[]{:S(2)}) copy-start(bf16[512,256]{0,1:T(8,128)(2,1)} %subtract_convert_fusion) | copy-start | bytes 786436
  170.7 11.4 %slice-start = ((pred[16384]{0:T(1024)(128)(4,1)}), pred[11264]{0:T(1024)(128)(4,1)S(1)}, s32[]{:S(2)}) async-start(pred[16384]{0:T(1024)(128)(4,1)} %copy-done.9), calls=%async_computation.3 | async-start | bytes 22528 | tf_op jit(solution)/shard_map/slice | solution.py:158
  180.7 37.2 %collective-permute-start.6 = (bf16[2,64,5120]{2,1,0:T(8,128)(2,1)}, bf16[2,64,5120]{2,1,0:T(8,128)(2,1)}, u32[]{:S(2)}, u32[]{:S(2)}) collective-permute-start(bf16[2,64,5120]{2,1,0:T(8,128)(2,1)} %bitcast_multiply_fusion.1), channel_id=1, source_target_pairs={{0,6},{2,0},{4,2},{6,4},{1,7},{3,1},{5,3},{7,5},{8,14},{10,8},{12,... | collective-permute-start | bytes 3932168 | tf_op jit(solution)/shard_map/ppermute | solution.py:13
  181.3 31.4 %collective-permute-start.7 = (bf16[2,64,5120]{2,1,0:T(8,128)(2,1)}, bf16[2,64,5120]{2,1,0:T(8,128)(2,1)}, u32[]{:S(2)}, u32[]{:S(2)}) collective-permute-start(bf16[2,64,5120]{2,1,0:T(8,128)(2,1)} %bitcast_multiply_fusion.1), channel_id=1, source_target_pairs={{0,2},{2,4},{4,6},{6,0},{1,3},{3,5},{5,7},{7,1},{8,10},{10,12},{12... | collective-permute-start | bytes 3932168 | tf_op jit(solution)/shard_map/ppermute | solution.py:13
  213.9 16.3 %collective-permute-start.8 = (bf16[2,32,5120]{2,1,0:T(8,128)(2,1)S(1)}, bf16[2,32,5120]{2,1,0:T(8,128)(2,1)S(1)}, u32[]{:S(2)}, u32[]{:S(2)}) collective-permute-start(bf16[2,32,5120]{2,1,0:T(8,128)(2,1)S(1)} %slice.346), channel_id=1, source_target_pairs={{0,2},{2,4},{4,6},{6,0},{1,3},{3,5},{5,7},{7,1},{8,10},{10,12},{12... | collective-permute-start | bytes 1966088 | tf_op jit(solution)/shard_map/ppermute | solution.py:13
  219.0 15.2 %collective-permute-start.9 = (bf16[2,32,5120]{2,1,0:T(8,128)(2,1)S(1)}, bf16[2,32,5120]{2,1,0:T(8,128)(2,1)S(1)}, u32[]{:S(2)}, u32[]{:S(2)}) collective-permute-start(bf16[2,32,5120]{2,1,0:T(8,128)(2,1)S(1)} %slice.347), channel_id=1, source_target_pairs={{0,6},{2,0},{4,2},{6,4},{1,7},{3,1},{5,3},{7,5},{8,14},{10,8},{12,... | collective-permute-start | bytes 1966088 | tf_op jit(solution)/shard_map/ppermute | solution.py:13
  223.3 12.6 %copy-start.11 = (pred[2560]{0:T(1024)(128)(4,1)S(1)}, pred[2560]{0:T(1024)(128)(4,1)}, u32[]{:S(2)}) copy-start(pred[2560]{0:T(1024)(128)(4,1)} %get-tuple-element.46) | copy-start | bytes 7684
  235.8 6.5 %copy-start.10 = (pred[2560]{0:T(1024)(128)(4,1)S(1)}, pred[2560]{0:T(1024)(128)(4,1)}, u32[]{:S(2)}) copy-start(pred[2560]{0:T(1024)(128)(4,1)} %get-tuple-element.47) | copy-start | bytes 7684
  239.6 16.9 %collective-permute-start.10 = (bf16[2,32,2560]{2,1,0:T(8,128)(2,1)S(1)}, bf16[2,32,2560]{2,1,0:T(8,128)(2,1)S(1)}, u32[]{:S(2)}, u32[]{:S(2)}) collective-permute-start(bf16[2,32,2560]{2,1,0:T(8,128)(2,1)S(1)} %get-tuple-element.38), channel_id=1, source_target_pairs={{0,8},{8,16},{16,24},{24,0},{32,40},{40,48},{48,56},{56,32},{64,72... | collective-permute-start | bytes 983048 | tf_op jit(solution)/shard_map/ppermute | solution.py:31
  240.6 16.3 %collective-permute-start.12 = (bf16[2,32,2560]{2,1,0:T(8,128)(2,1)S(1)}, bf16[2,32,2560]{2,1,0:T(8,128)(2,1)S(1)}, u32[]{:S(2)}, u32[]{:S(2)}) collective-permute-start(bf16[2,32,2560]{2,1,0:T(8,128)(2,1)S(1)} %get-tuple-element.39), channel_id=1, source_target_pairs={{0,24},{8,0},{16,8},{24,16},{32,56},{40,32},{48,40},{56,48},{64,88... | collective-permute-start | bytes 983048 | tf_op jit(solution)/shard_map/ppermute | solution.py:31
  245.9 14.8 %collective-permute-start.18 = (bf16[2,32,2560]{2,1,0:T(8,128)(2,1)S(1)}, bf16[2,32,2560]{2,1,0:T(8,128)(2,1)S(1)}, u32[]{:S(2)}, u32[]{:S(2)}) collective-permute-start(bf16[2,32,2560]{2,1,0:T(8,128)(2,1)S(1)} %get-tuple-element.40), channel_id=1, source_target_pairs={{0,32},{8,40},{16,48},{24,56},{32,64},{40,72},{48,80},{56,88},{64,... | collective-permute-start | bytes 983048 | tf_op jit(solution)/shard_map/ppermute | solution.py:31
  247.0 13.7 %collective-permute-start.20 = (bf16[2,32,2560]{2,1,0:T(8,128)(2,1)S(1)}, bf16[2,32,2560]{2,1,0:T(8,128)(2,1)S(1)}, u32[]{:S(2)}, u32[]{:S(2)}) collective-permute-start(bf16[2,32,2560]{2,1,0:T(8,128)(2,1)S(1)} %get-tuple-element.41), channel_id=1, source_target_pairs={{0,96},{8,104},{16,112},{24,120},{32,0},{40,8},{48,16},{56,24},{64... | collective-permute-start | bytes 983048 | tf_op jit(solution)/shard_map/ppermute | solution.py:31
  256.7 24.0 %collective-permute-start.11 = (bf16[4,32,2560]{2,1,0:T(8,128)(2,1)S(1)}, bf16[4,32,2560]{2,1,0:T(8,128)(2,1)S(1)}, u32[]{:S(2)}, u32[]{:S(2)}) collective-permute-start(bf16[4,32,2560]{2,1,0:T(8,128)(2,1)S(1)} %pad_maximum_fusion), channel_id=1, source_target_pairs={{0,8},{8,16},{16,24},{24,0},{32,40},{40,48},{48,56},{56,32},{64,72... | collective-permute-start | bytes 1966088 | tf_op jit(solution)/shard_map/ppermute | solution.py:31
  257.1 23.5 %collective-permute-start.13 = (bf16[4,32,2560]{2,1,0:T(8,128)(2,1)S(1)}, bf16[4,32,2560]{2,1,0:T(8,128)(2,1)S(1)}, u32[]{:S(2)}, u32[]{:S(2)}) collective-permute-start(bf16[4,32,2560]{2,1,0:T(8,128)(2,1)S(1)} %pad_maximum_fusion.1), channel_id=1, source_target_pairs={{0,24},{8,0},{16,8},{24,16},{32,56},{40,32},{48,40},{56,48},{64,88... | collective-permute-start | bytes 1966088 | tf_op jit(solution)/shard_map/ppermute | solution.py:31
  260.9 22.8 %collective-permute-start.19 = (bf16[4,32,2560]{2,1,0:T(8,128)(2,1)S(1)}, bf16[4,32,2560]{2,1,0:T(8,128)(2,1)S(1)}, u32[]{:S(2)}, u32[]{:S(2)}) collective-permute-start(bf16[4,32,2560]{2,1,0:T(8,128)(2,1)S(1)} %pad_maximum_fusion.2), channel_id=1, source_target_pairs={{0,32},{8,40},{16,48},{24,56},{32,64},{40,72},{48,80},{56,88},{64,... | collective-permute-start | bytes 1966088 | tf_op jit(solution)/shard_map/ppermute | solution.py:31
  261.9 21.8 %collective-permute-start.21 = (bf16[4,32,2560]{2,1,0:T(8,128)(2,1)S(1)}, bf16[4,32,2560]{2,1,0:T(8,128)(2,1)S(1)}, u32[]{:S(2)}, u32[]{:S(2)}) collective-permute-start(bf16[4,32,2560]{2,1,0:T(8,128)(2,1)S(1)} %pad_maximum_fusion.3), channel_id=1, source_target_pairs={{0,96},{8,104},{16,112},{24,120},{32,0},{40,8},{48,16},{56,24},{64... | collective-permute-start | bytes 1966088 | tf_op jit(solution)/shard_map/ppermute | solution.py:31
  280.9 5.9 %collective-permute-start.14 = (bf16[16,2560]{1,0:T(8,128)(2,1)S(1)}, bf16[16,2560]{1,0:T(8,128)(2,1)S(1)}, u32[]{:S(2)}, u32[]{:S(2)}) collective-permute-start(bf16[16,2560]{1,0:T(8,128)(2,1)S(1)} %get-tuple-element.42), channel_id=1, source_target_pairs={{0,32},{8,40},{16,48},{24,56},{32,64},{40,72},{48,80},{56,88},{64,... | collective-permute-start | bytes 245768 | tf_op jit(solution)/shard_map/ppermute | solution.py:31
  281.0 5.8 %collective-permute-start.16 = (bf16[16,2560]{1,0:T(8,128)(2,1)S(1)}, bf16[16,2560]{1,0:T(8,128)(2,1)S(1)}, u32[]{:S(2)}, u32[]{:S(2)}) collective-permute-start(bf16[16,2560]{1,0:T(8,128)(2,1)S(1)} %get-tuple-element.43), channel_id=1, source_target_pairs={{0,96},{8,104},{16,112},{24,120},{32,0},{40,8},{48,16},{56,24},{64... | collective-permute-start | bytes 245768 | tf_op jit(solution)/shard_map/ppermute | solution.py:31
  284.1 6.5 %collective-permute-start.22 = (bf16[16,2560]{1,0:T(8,128)(2,1)S(1)}, bf16[16,2560]{1,0:T(8,128)(2,1)S(1)}, u32[]{:S(2)}, u32[]{:S(2)}) collective-permute-start(bf16[16,2560]{1,0:T(8,128)(2,1)S(1)} %get-tuple-element.44), channel_id=1, source_target_pairs={{0,8},{8,16},{16,24},{24,0},{32,40},{40,48},{48,56},{56,32},{64,72... | collective-permute-start | bytes 245768 | tf_op jit(solution)/shard_map/ppermute | solution.py:31
  284.4 6.2 %collective-permute-start.24 = (bf16[16,2560]{1,0:T(8,128)(2,1)S(1)}, bf16[16,2560]{1,0:T(8,128)(2,1)S(1)}, u32[]{:S(2)}, u32[]{:S(2)}) collective-permute-start(bf16[16,2560]{1,0:T(8,128)(2,1)S(1)} %get-tuple-element.45), channel_id=1, source_target_pairs={{0,24},{8,0},{16,8},{24,16},{32,56},{40,32},{48,40},{56,48},{64,88... | collective-permute-start | bytes 245768 | tf_op jit(solution)/shard_map/ppermute | solution.py:31
  286.9 9.8 %collective-permute-start.15 = (bf16[32,2560]{1,0:T(8,128)(2,1)S(1)}, bf16[32,2560]{1,0:T(8,128)(2,1)S(1)}, u32[]{:S(2)}, u32[]{:S(2)}) collective-permute-start(bf16[32,2560]{1,0:T(8,128)(2,1)S(1)} %pad_maximum_fusion.10), channel_id=1, source_target_pairs={{0,32},{8,40},{16,48},{24,56},{32,64},{40,72},{48,80},{56,88},{64,... | collective-permute-start | bytes 491528 | tf_op jit(solution)/shard_map/ppermute | solution.py:31
  287.0 9.7 %collective-permute-start.17 = (bf16[32,2560]{1,0:T(8,128)(2,1)S(1)}, bf16[32,2560]{1,0:T(8,128)(2,1)S(1)}, u32[]{:S(2)}, u32[]{:S(2)}) collective-permute-start(bf16[32,2560]{1,0:T(8,128)(2,1)S(1)} %pad_maximum_fusion.11), channel_id=1, source_target_pairs={{0,96},{8,104},{16,112},{24,120},{32,0},{40,8},{48,16},{56,24},{64... | collective-permute-start | bytes 491528 | tf_op jit(solution)/shard_map/ppermute | solution.py:31
  290.7 9.3 %collective-permute-start.23 = (bf16[32,2560]{1,0:T(8,128)(2,1)S(1)}, bf16[32,2560]{1,0:T(8,128)(2,1)S(1)}, u32[]{:S(2)}, u32[]{:S(2)}) collective-permute-start(bf16[32,2560]{1,0:T(8,128)(2,1)S(1)} %pad_maximum_fusion.12), channel_id=1, source_target_pairs={{0,8},{8,16},{16,24},{24,0},{32,40},{40,48},{48,56},{56,32},{64,72... | collective-permute-start | bytes 491528 | tf_op jit(solution)/shard_map/ppermute | solution.py:31
  290.8 9.2 %collective-permute-start.25 = (bf16[32,2560]{1,0:T(8,128)(2,1)S(1)}, bf16[32,2560]{1,0:T(8,128)(2,1)S(1)}, u32[]{:S(2)}, u32[]{:S(2)}) collective-permute-start(bf16[32,2560]{1,0:T(8,128)(2,1)S(1)} %pad_maximum_fusion.13), channel_id=1, source_target_pairs={{0,24},{8,0},{16,8},{24,16},{32,56},{40,32},{48,40},{56,48},{64,88... | collective-permute-start | bytes 491528 | tf_op jit(solution)/shard_map/ppermute | solution.py:31
Sparse Core Ops, SparseCore 0:
  198.2 105.8 reduce-scatter.1
